TPU v7x, 128 devices: a whole 4x4x4 slice. The times are simulated.
128 devices in a mesh: req: 16 (over y, z_hi, core), kv: 8 (over z_lo, x).
Axes of the slice: x: 4, y: 4, z: 4 (z_hi: 2, z_lo: 2; z = z_hi * 2 + z_lo), core: 2. Of those that a mesh axis runs over, the one named last changes fastest.
Arguments:
- tokens: bfloat16 [1024, 8192], P(None, 'req'), may hold values from -40 to 40
- norm_in: bfloat16 [8192], P('req'), may hold values from 0.099609375 to 1.8984375
- w_qkv: bfloat16 [8192, 10240], P('req', 'kv'), may hold values from -0.0625 to 0.0625
- qkv_bias: bfloat16 [10240], P('kv'), may hold values from -12 to 12
- w_out: bfloat16 [8192, 8192], P('kv', 'req'), may hold values from -0.0625 to 0.0625
- norm_mid: bfloat16 [8192], P('req'), may hold values from 0.099609375 to 1.8984375
- w_gate: bfloat16 [8192, 29568], P('req', 'kv'), may hold values from -0.0625 to 0.0625
- w_up: bfloat16 [8192, 29568], P('req', 'kv'), may hold values from -0.0625 to 0.0625
- w_down: bfloat16 [29568, 8192], P('kv', 'req'), may hold values from -0.03125 to 0.03125
- short_keys: bfloat16 [1024, 256, 8, 128], P('req', None, 'kv'), may hold values from -310 to 310
- short_values: bfloat16 [1024, 256, 8, 128], P('req', None, 'kv'), may hold values from -6 to 6
- short_len: int32 [1024], P('req'), may hold values from 1 to 256, 131072 in all
- long_keys: bfloat16 [16, 8192, 8, 128], P('req', None, 'kv'), may hold values from -310 to 310
- long_values: bfloat16 [16, 8192, 8, 128], P('req', None, 'kv'), may hold values from -6 to 6
- long_len: int32 [16], replicated, may hold values from 0 to 8192, as said below
- positions: int32 [1024], P('req'), may hold values from 0 to 32767
Outputs:
- layer_out: bfloat16 [1024, 8192], P(None, 'req')
Inputs may be any that keep to these rules, and one draw needn't show every extreme that they name: `short_len`: short lengths sum to 131072 and the largest is 256. `long_len`: exactly 8 segments are live, the others have length 0; live ones hold at least 4096 slots and one holds 8192.
All inputs are finite; a program needn't handle non-finite values. No bound on the sum of `short_len` on one device may be relied on, other than what follows from the above.
Results may differ from a plain program's by a relative error of at most 0.0085.
Values may be sent and summed in bfloat16 or wider, within the bound.
No kernel may reach another device: no remote copies, remote signals or barrier semaphores. Data moves between devices by JAX's collectives and lax.ppermute only.
A program may use at most 128 MiB of HBM per device.

v0:
```python
import jax
import jax.numpy as jnp
from jax import lax
from jax.sharding import PartitionSpec as P

D = 8192
HD = 128
SHORT_CAP = 256
LONG_CAP = 8192
REQ_DEV = 64
GROUP = 8
EPS = 1e-06
THETA = 1000000.0
NEGATIVE = -1e30


def rotate(values, angles):
    half = values.shape[-1] // 2
    first = values[..., :half]
    second = values[..., half:]
    cosine = jnp.cos(angles)
    sine = jnp.sin(angles)
    return jnp.concatenate(
        [first * cosine - second * sine, second * cosine + first * sine], axis=-1
    )


def weigh(short_raw, own_raw, short_values, own_values, peak):
    short_weights = jnp.exp(short_raw - peak[..., None])
    own_weights = jnp.exp(own_raw - peak)
    total = jnp.sum(short_weights, axis=3) + own_weights
    summed = jnp.einsum(
        "rhgs,rshd->rhgd",
        short_weights.astype(jnp.bfloat16),
        short_values,
        preferred_element_type=jnp.float32,
    )
    summed = summed + jnp.einsum(
        "rhg,rhd->rhgd",
        own_weights.astype(jnp.bfloat16),
        own_values,
        preferred_element_type=jnp.float32,
    )
    return (total, summed)


def per_device(
    tokens,
    norm_in,
    w_qkv,
    qkv_bias,
    w_out,
    norm_mid,
    w_gate,
    w_up,
    w_down,
    short_keys,
    short_values,
    short_len,
    long_keys,
    long_values,
    long_len,
    positions,
):
    heads_here = short_keys.shape[2]
    scale = HD ** (-0.5)
    wide = tokens.astype(jnp.float32)
    slot = lax.axis_index("req")
    square_in = lax.psum(jnp.sum(wide * wide, axis=1), "req")
    gained = (wide * norm_in.astype(jnp.float32)[None, :]).astype(jnp.bfloat16)
    united = lax.psum_scatter(
        jnp.dot(gained, w_qkv, preferred_element_type=jnp.float32).astype(jnp.bfloat16),
        "req",
        scatter_dimension=0,
        tiled=True,
    ).astype(jnp.float32)
    scale_in = lax.rsqrt(lax.dynamic_slice_in_dim(square_in, slot * REQ_DEV, REQ_DEV) / D + EPS)
    united = (united * scale_in[:, None] + qkv_bias.astype(jnp.float32)[None, :]).reshape(
        REQ_DEV, heads_here, GROUP + 2, HD
    )
    inv_freq = THETA ** (-(2.0 * jnp.arange(HD // 2, dtype=jnp.float32)) / HD)
    angles = positions.astype(jnp.float32)[:, None] * inv_freq[None, :]
    queries = rotate(united[:, :, :GROUP], angles[:, None, None, :]).astype(jnp.bfloat16)
    new_keys = rotate(united[:, :, GROUP], angles[:, None, :]).astype(jnp.bfloat16)
    new_values = united[:, :, GROUP + 1].astype(jnp.bfloat16)
    short_raw = (
        jnp.einsum("rhgd,rshd->rhgs", queries, short_keys, preferred_element_type=jnp.float32)
        * scale
    )
    live = jnp.arange(SHORT_CAP)[None, :] < short_len[:, None]
    short_raw = jnp.where(live[:, None, None, :], short_raw, NEGATIVE)
    own_raw = (
        jnp.einsum("rhgd,rhd->rhg", queries, new_keys, preferred_element_type=jnp.float32) * scale
    )
    peak = jnp.maximum(jnp.max(short_raw, axis=3), own_raw)
    slot_len = lax.dynamic_index_in_dim(long_len, slot, 0, keepdims=False)
    long_raw = (
        jnp.einsum("hgd,lhd->hgl", queries[0], long_keys[0], preferred_element_type=jnp.float32)
        * scale
    )
    long_live = jnp.arange(LONG_CAP) < slot_len
    long_raw = jnp.where(long_live[None, None, :], long_raw, NEGATIVE)
    first_peak = jnp.maximum(peak[0], jnp.max(long_raw, axis=2))
    peak = jnp.concatenate([first_peak[None], peak[1:]], axis=0)
    total, summed = weigh(short_raw, own_raw, short_values, new_values, peak)
    long_weights = jnp.where(
        long_live[None, None, :], jnp.exp(long_raw - first_peak[:, :, None]), 0.0
    )
    long_summed = jnp.einsum(
        "hgl,lhd->hgd",
        long_weights.astype(jnp.bfloat16),
        long_values[0],
        preferred_element_type=jnp.float32,
    )
    total = total.at[0].add(jnp.sum(long_weights, axis=2))
    summed = summed.at[0].add(long_summed)
    attended = (
        (summed / total[..., None]).astype(jnp.bfloat16).reshape(REQ_DEV, heads_here * GROUP * HD)
    )
    out_part = jnp.dot(
        lax.all_gather(attended, "req", axis=0, tiled=True),
        w_out,
        preferred_element_type=jnp.float32,
    )
    projected = lax.psum(out_part.astype(jnp.bfloat16), "kv").astype(jnp.float32)
    residual = lax.optimization_barrier((wide + projected).astype(jnp.bfloat16))
    resid_wide = residual.astype(jnp.float32)
    square_mid = lax.psum(jnp.sum(resid_wide * resid_wide, axis=1), "req")
    mixed_in = (resid_wide * norm_mid.astype(jnp.float32)[None, :]).astype(jnp.bfloat16)
    units = w_gate.shape[1]
    padded = -(-units // 128) * 128
    w_gate_up = jnp.concatenate(
        [
            jnp.pad(w_gate, ((0, 0), (0, padded - units))),
            jnp.pad(w_up, ((0, 0), (0, padded - units))),
        ],
        axis=1,
    )
    gate_up = lax.psum_scatter(
        jnp.dot(mixed_in, w_gate_up, preferred_element_type=jnp.float32).astype(jnp.bfloat16),
        "req",
        scatter_dimension=0,
        tiled=True,
    ).astype(jnp.float32)
    scale_mid = lax.rsqrt(lax.dynamic_slice_in_dim(square_mid, slot * REQ_DEV, REQ_DEV) / D + EPS)
    gate = gate_up[:, :units] * scale_mid[:, None]
    up = gate_up[:, padded : padded + units] * scale_mid[:, None]
    act = (jax.nn.silu(gate) * up).astype(jnp.bfloat16)
    down_part = jnp.dot(
        lax.all_gather(act, "req", axis=0, tiled=True), w_down, preferred_element_type=jnp.float32
    )
    down = lax.psum(down_part.astype(jnp.bfloat16), "kv").astype(jnp.float32)
    return (resid_wide + down).astype(jnp.bfloat16)


def solution(mesh):
    placed = (
        P(None, "req"),
        P("req"),
        P("req", "kv"),
        P("kv"),
        P("kv", "req"),
        P("req"),
        P("req", "kv"),
        P("req", "kv"),
        P("kv", "req"),
        P("req", None, "kv", None),
        P("req", None, "kv", None),
        P("req"),
        P("req", None, "kv", None),
        P("req", None, "kv", None),
        P(),
        P("req"),
    )
    return jax.shard_map(
        per_device, mesh=mesh, in_specs=placed, out_specs=P(None, "req"), check_vma=False
    )
```

profile of v0, /device:TPU:0, one launch (start us, length us, event | category | flops | bytes accessed | tf_op | source)
XLA Modules:
  0.0 543.8 jit_solution(6019344185695769220)
XLA Ops:
  6.5 0.8 convert_element_type.96
  7.4 4.8 convolution_convert_fusion.1
  12.2 0.0 all-gather.3.cloned.1.call-start
  12.3 0.6 dynamic_slice.11
  12.9 0.3 fusion.15
  13.2 39.1 %psum.28 = f32[1024]{0:T(1024)S(1)} all-reduce(f32[1024]{0:T(1024)S(1)} %fusion.15), channel_id=1, replica_groups=mesh['req'=16,'kv'=8] {'req'}, use_global_device_ids=true, to_apply=%region_2.0 | all-reduce | flops 1024 | bytes 8192 | tf_op jit(solution)/shard_map/psum | solution.py:69
  52.3 0.1 add_rsqrt_fusion.1
  52.4 0.7 iota_compare_fusion.3
  53.1 0.1 iota_compare_fusion.2
  53.1 0.2 multiply_cosine_fusion.1
  53.3 35.0 %reduce-scatter.3.cloned.1.call-done = bf16[64,1280]{1,0:T(8,128)(2,1)} async-done(((bf16[1024,1280]{1,0:T(8,128)(2,1)}), bf16[64,1280]{1,0:T(8,128)(2,1)}) %reduce-scatter.3.cloned.1.call-update) | async-done | bytes 163856 | tf_op jit(solution)/shard_map/reduce_scatter | solution.py:71
  88.3 1.0 multiply_add_fusion
  89.3 0.1 reshape.419
  89.5 0.2 fusion.70
  89.7 0.1 maximum_bitcast_fusion
  89.7 0.2 subtract_convert_fusion
  89.9 0.8 fusion.84
  90.7 0.3 fusion.67
  91.0 3.5 fusion.83
  94.6 0.1 copy.28
  94.7 0.1 copy.29
  94.7 0.1 maximum_bitcast_fusion.1
  94.8 0.1 copy.30
  94.9 0.3 fusion.51
  95.2 0.2 fusion.47
  95.5 2.9 fusion.29
  98.4 2.0 fusion.38
  100.4 0.1 divide_convert_fusion
  100.6 0.7 copy.38
  101.3 0.0 all-reduce.5.cloned.1.call-start
  101.4 47.1 %all-gather.3.cloned.1.call-done = bf16[1024,1024]{1,0:T(8,128)(2,1)} async-done(((bf16[64,1024]{1,0:T(8,128)(2,1)}), bf16[1024,1024]{1,0:T(8,128)(2,1)}) %all-gather.3.cloned.1.call-update) | async-done | bytes 2097168 | tf_op jit(solution)/shard_map/all_gather | solution.py:121
  148.5 4.1 convolution_convert_fusion.3
  152.6 0.0 reduce-scatter.5.cloned.1.call-start
  152.6 76.1 %all-reduce.5.cloned.1.call-done = bf16[1024,512]{1,0:T(8,128)(2,1)} async-done(((bf16[1024,512]{1,0:T(8,128)(2,1)}), bf16[1024,512]{1,0:T(8,128)(2,1)}) %all-reduce.5.cloned.1.call-update) | async-done | bytes 1048592 | tf_op jit(solution)/shard_map/psum | solution.py:125
  228.8 1.5 fusion.16
  230.3 14.7 %convolution_convert_fusion = bf16[1024,7424]{1,0:T(8,128)(2,1)} fusion(bf16[512,3696]{0,1:T(8,128)(2,1)} %param.27, bf16[512,3696]{0,1:T(8,128)(2,1)} %param.26, bf16[1024,512]{1,0:T(8,128)(2,1)S(1)} %fusion.16, f32[512]{0:T(512)S(1)} %convert_element_type.110), kind=kOutput, calls=%fused_computation.4 | convolution fusion | flops 7824211968 | bytes 23824384 | tf_op jit(solution)/shard_map/dot_general | solution.py:140
  245.0 0.0 all-gather.5.cloned.1.call-start
  245.0 0.3 fusion.18
  245.3 33.3 %psum.30 = f32[1024]{0:T(1024)S(1)} all-reduce(f32[1024]{0:T(1024)S(1)} %fusion.18), channel_id=1, replica_groups=mesh['req'=16,'kv'=8] {'req'}, use_global_device_ids=true, to_apply=%region_10.11 | all-reduce | flops 1024 | bytes 8192 | tf_op jit(solution)/shard_map/psum | solution.py:128
  278.7 0.1 add_rsqrt_fusion
  278.7 101.1 %reduce-scatter.5.cloned.1.call-done = bf16[64,7424]{1,0:T(8,128)(2,1)} async-done(((bf16[1024,7424]{1,0:T(8,128)(2,1)}), bf16[64,7424]{1,0:T(8,128)(2,1)}) %reduce-scatter.5.cloned.1.call-update) | async-done | bytes 950288 | tf_op jit(solution)/shard_map/reduce_scatter | solution.py:139
  379.8 1.3 convert_element_type.113
  381.1 1.1 fusion.46
  382.3 0.0 all-reduce.7.cloned.1.call-start
  382.3 67.5 %all-gather.5.cloned.1.call-done = bf16[1024,3696]{1,0:T(8,128)(2,1)} async-done(((bf16[64,3696]{1,0:T(8,128)(2,1)}), bf16[1024,3696]{1,0:T(8,128)(2,1)}) %all-gather.5.cloned.1.call-update) | async-done | bytes 7569424 | tf_op jit(solution)/shard_map/all_gather | solution.py:150
  449.8 9.6 %convolution_convert_fusion.2 = bf16[1024,512]{1,0:T(8,128)(2,1)} fusion(bf16[1024,3696]{1,0:T(8,128)(2,1)} %all-gather.5.cloned.1.call-done, bf16[3696,512]{1,0:T(8,128)(2,1)} %param.28), kind=kOutput, calls=%fused_computation.32 | convolution fusion | flops 3876061184 | bytes 12402688 | tf_op jit(solution)/shard_map/dot_general | solution.py:149
  459.4 75.1 %all-reduce.7.cloned.1.call-done = bf16[1024,512]{1,0:T(8,128)(2,1)} async-done(((bf16[1024,512]{1,0:T(8,128)(2,1)}), bf16[1024,512]{1,0:T(8,128)(2,1)}) %all-reduce.7.cloned.1.call-update) | async-done | bytes 1048592 | tf_op jit(solution)/shard_map/psum | solution.py:152
  534.5 2.5 fusion.19
  (40 shorter events, 0.3 us)
Async XLA Ops:
  6.5 83.4 %copy-start = (bf16[1,8192,1,128]{3,1,2,0:T(8,128)(2,1)S(1)}, bf16[1,8192,1,128]{3,1,2,0:T(8,128)(2,1)}, u32[]{:S(2)}) copy-start(bf16[1,8192,1,128]{3,1,2,0:T(8,128)(2,1)} %param.32) | copy-start | bytes 6291460
  6.5 81.8 %reduce-scatter.3.cloned.1.call-start = ((), (), s32[]{:S(2)}) async-start(), calls=%async_computation.2 | async-start | bytes 2785280 | tf_op jit(solution)/shard_map/reduce_scatter | solution.py:71
  7.4 4.9 copy-start.7
  7.4 4.9 copy-start.4
  7.4 4.9 copy-start.8
  7.4 5.5 %copy-start.2 = (bf16[1024,512]{1,0:T(8,128)(2,1)S(1)}, bf16[1024,512]{1,0:T(8,128)(2,1)}, u32[]{:S(2)}) copy-start(bf16[1024,512]{1,0:T(8,128)(2,1)} %param.20) | copy-start | bytes 3145732
  7.4 45.7 %copy-start.6 = (s32[64]{0:T(128)S(1)}, s32[64]{0:T(128)}, u32[]{:S(2)}) copy-start(s32[64]{0:T(128)} %param.31) | copy-start | bytes 772
  12.2 136.3 %all-gather.3.cloned.1.call-start = ((), (), s32[]{:S(2)}) async-start(), calls=%async_computation.3 | async-start | bytes 2228224 | tf_op jit(solution)/shard_map/all_gather | solution.py:121
  101.3 51.3 %copy-start.5 = (bf16[512]{0:T(512)(128)(2,1)S(1)}, bf16[512]{0:T(512)(128)(2,1)}, u32[]{:S(2)}) copy-start(bf16[512]{0:T(512)(128)(2,1)} %param.25) | copy-start | bytes 3076
  101.3 127.5 %copy-start.3 = (bf16[1024,512]{1,0:T(8,128)(2,1)S(1)}, bf16[1024,512]{1,0:T(8,128)(2,1)}, u32[]{:S(2)}) copy-start(bf16[1024,512]{1,0:T(8,128)(2,1)} %param.20) | copy-start | bytes 3145732
  101.3 127.4 %all-reduce.5.cloned.1.call-start = ((), (), s32[]{:S(2)}) async-start(), calls=%async_computation.4 | async-start | bytes 2097152 | tf_op jit(solution)/shard_map/psum | solution.py:125
  152.6 227.3 %reduce-scatter.5.cloned.1.call-start = ((), (), s32[]{:S(2)}) async-start(), calls=%async_computation.5 | async-start | bytes 16154624 | tf_op jit(solution)/shard_map/reduce_scatter | solution.py:139
  245.0 204.8 %all-gather.5.cloned.1.call-start = ((), (), s32[]{:S(2)}) async-start(), calls=%async_computation.6 | async-start | bytes 8077312 | tf_op jit(solution)/shard_map/all_gather | solution.py:150
  382.3 152.2 %all-reduce.7.cloned.1.call-start = ((), (), s32[]{:S(2)}) async-start(), calls=%async_computation.7 | async-start | bytes 2097152 | tf_op jit(solution)/shard_map/psum | solution.py:152
  449.8 87.2 %copy-start.1 = (bf16[1,8192,1,128]{3,1,2,0:T(8,128)(2,1)S(1)}, bf16[1,8192,1,128]{3,1,2,0:T(8,128)(2,1)}, u32[]{:S(2)}) copy-start(bf16[1,8192,1,128]{3,1,2,0:T(8,128)(2,1)} %param.32) | copy-start | bytes 6291460
Sparse Core Ops, SparseCore 0:
  12.3 75.9 reduce-scatter.2
  101.4 47.0 all-gather.2
  152.7 76.0 all-reduce.4
  245.1 134.6 reduce-scatter.4
  382.4 67.3 all-gather.4
  459.5 74.9 all-reduce.6
where the time goes:
time: 544 us
  waiting for transfers between devices  402 us (74%)
  blocking collectives  72.5 us (13%)
  matrix products  42.6 us (8%)
  between operations  13.8 us (3%)
  other arithmetic  11.2 us (2%)
    reduce_scatter x1, waiting for transfers between devices, per_device(): lax.psum_scatter(jnp.dot(mixed_in, w_gate_up, preferred_element_type=jnp....  101 us
    psum x1, waiting for transfers between devices, per_device(): lax.psum(out_part.astype(jnp.bfloat16), 'kv').astype(jnp.float32)  76.1 us
    psum x1, waiting for transfers between devices, per_device(): down = lax.psum(down_part.astype(jnp.bfloat16), 'kv').astype(jnp.float32)  75.1 us
    all_gather x1, waiting for transfers between devices, per_device(): lax.all_gather(act, 'req', axis=0, tiled=True)  67.5 us
    all_gather x1, waiting for transfers between devices, per_device(): lax.all_gather(attended, 'req', axis=0, tiled=True)  47.1 us
    psum x1, blocking collectives, per_device(): square_in = lax.psum(jnp.sum(wide * wide, axis=1), 'req')  39.1 us
    reduce_scatter x1, waiting for transfers between devices, per_device(): lax.psum_scatter(jnp.dot(gained, w_qkv, preferred_element_type=jnp.float3...  35 us
    psum x1, blocking collectives, per_device(): square_mid = lax.psum(jnp.sum(resid_wide * resid_wide, axis=1), 'req')  33.3 us
  transfers between devices with their start and end apart: 6, of which 6 were waited for; matrix products, arithmetic and copies ran while one was open for 0% of the time, Pallas kernels for 0%

commit v1 on v0

--- a/solution.py
+++ b/solution.py
@@ -118,7 +118,9 @@
         (summed / total[..., None]).astype(jnp.bfloat16).reshape(REQ_DEV, heads_here * GROUP * HD)
     )
     out_part = jnp.dot(
-        lax.all_gather(attended, "req", axis=0, tiled=True),
+        jnp.concatenate(
+            lax.all_to_all(jnp.stack([attended] * lax.axis_size("req")), "req", 0, 0), axis=0
+        ),
         w_out,
         preferred_element_type=jnp.float32,
     )

time: 544 us -> 526 us (0.967)
  waiting for transfers between devices: 402 us -> 353 us
  blocking collectives: 72.5 us -> 106 us
    all_gather x1 -> x0, waiting for transfers between devices: 47.1 us -> none  [per_device(): lax.all_gather(attended, 'req', axis=0, tiled=True)]
    all_to_all x0 -> x1, blocking collectives: none -> 33.5 us  [per_device(): lax.all_to_all(jnp.stack([attended] * lax.axis_size('req')), 'req', 0, 0)]
  transfers between devices with their start and end apart: 6 -> 5, of which waited for: 6 -> 5; matrix products, arithmetic and copies ran while one was open for 0% -> 0% of each run, Pallas kernels for 0% -> 0%
where the time goes in v1:
time: 526 us
  waiting for transfers between devices  353 us (67%)
  blocking collectives  106 us (20%)
  matrix products  40.7 us (8%)
  between operations  13.4 us (3%)
  other arithmetic  11.2 us (2%)
    reduce_scatter x1, waiting for transfers between devices, per_device(): lax.psum_scatter(jnp.dot(mixed_in, w_gate_up, preferred_element_type=jnp....  101 us
    psum x1, waiting for transfers between devices, per_device(): down = lax.psum(down_part.astype(jnp.bfloat16), 'kv').astype(jnp.float32)  75.1 us
    psum x1, waiting for transfers between devices, per_device(): lax.psum(out_part.astype(jnp.bfloat16), 'kv').astype(jnp.float32)  74.2 us
    all_gather x1, waiting for transfers between devices, per_device(): lax.all_gather(act, 'req', axis=0, tiled=True)  67.5 us
    psum x1, blocking collectives, per_device(): square_in = lax.psum(jnp.sum(wide * wide, axis=1), 'req')  39.1 us
    reduce_scatter x1, waiting for transfers between devices, per_device(): lax.psum_scatter(jnp.dot(gained, w_qkv, preferred_element_type=jnp.float3...  35 us
    all_to_all x1, blocking collectives, per_device(): lax.all_to_all(jnp.stack([attended] * lax.axis_size('req')), 'req', 0, 0)  33.5 us
    psum x1, blocking collectives, per_device(): square_mid = lax.psum(jnp.sum(resid_wide * resid_wide, axis=1), 'req')  33.2 us
  transfers between devices with their start and end apart: 5, of which 5 were waited for; matrix products, arithmetic and copies ran while one was open for 0% of the time, Pallas kernels for 0%

profile of v1, /device:TPU:0, one launch (start us, length us, event | category | flops | bytes accessed | tf_op | source)
XLA Modules:
  0.0 525.6 jit_solution(1256387426290898459)
XLA Ops:
  6.5 0.8 convert_element_type.96
  7.4 4.8 convolution_convert_fusion.1
  12.2 0.0 reduce-scatter.3.cloned.1.call-update
  12.2 0.0 all-reduce.5.cloned.1.call-start
  12.3 0.6 dynamic_slice.11
  12.9 0.3 fusion.15
  13.2 39.1 %psum.28 = f32[1024]{0:T(1024)S(1)} all-reduce(f32[1024]{0:T(1024)S(1)} %fusion.15), channel_id=1, replica_groups=mesh['req'=16,'kv'=8] {'req'}, use_global_device_ids=true, to_apply=%region_2.0 | all-reduce | flops 1024 | bytes 8192 | tf_op jit(solution)/shard_map/psum | solution.py:69
  52.3 0.1 add_rsqrt_fusion.1
  52.4 0.7 iota_compare_fusion.3
  53.1 0.1 iota_compare_fusion.2
  53.1 0.2 multiply_cosine_fusion.1
  53.3 35.0 %reduce-scatter.3.cloned.1.call-done = bf16[64,1280]{1,0:T(8,128)(2,1)} async-done(((bf16[1024,1280]{1,0:T(8,128)(2,1)}), bf16[64,1280]{1,0:T(8,128)(2,1)}) %reduce-scatter.3.cloned.1.call-update) | async-done | bytes 163856 | tf_op jit(solution)/shard_map/reduce_scatter | solution.py:71
  88.3 1.0 multiply_add_fusion
  89.3 0.1 reshape.421
  89.5 0.2 fusion.70
  89.7 0.1 maximum_bitcast_fusion
  89.7 0.2 subtract_convert_fusion
  89.9 0.8 fusion.84
  90.7 0.3 fusion.67
  91.0 3.5 fusion.83
  94.6 0.1 copy.28
  94.7 0.1 copy.29
  94.7 0.1 maximum_bitcast_fusion.1
  94.8 0.1 copy.30
  94.9 0.3 fusion.51
  95.2 0.2 fusion.47
  95.5 2.9 fusion.29
  98.4 2.0 fusion.38
  100.4 0.2 divide_convert_fusion
  100.6 0.3 stack.3
  100.9 33.5 %all_to_all.5 = bf16[16,64,1024]{2,1,0:T(8,128)(2,1)S(1)} all-to-all(bf16[16,64,1024]{2,1,0:T(8,128)(2,1)S(1)} %stack.3), channel_id=1, replica_groups=mesh['req'=16,'kv'=8] {'req'}, dimensions={0} | all-to-all | bytes 4194304 | tf_op jit(solution)/shard_map/all_to_all | solution.py:122
  134.4 2.2 convolution_convert_fusion.3
  136.6 0.0 reduce-scatter.5.cloned.1.call-start
  136.7 74.2 %all-reduce.5.cloned.1.call-done = bf16[1024,512]{1,0:T(8,128)(2,1)} async-done(((bf16[1024,512]{1,0:T(8,128)(2,1)}), bf16[1024,512]{1,0:T(8,128)(2,1)}) %all-reduce.5.cloned.1.call-update) | async-done | bytes 1048592 | tf_op jit(solution)/shard_map/psum | solution.py:127
  210.9 1.5 fusion.16
  212.4 14.7 %convolution_convert_fusion = bf16[1024,7424]{1,0:T(8,128)(2,1)} fusion(bf16[512,3696]{0,1:T(8,128)(2,1)} %param.27, bf16[512,3696]{0,1:T(8,128)(2,1)} %param.26, bf16[1024,512]{1,0:T(8,128)(2,1)S(1)} %fusion.16, f32[512]{0:T(512)S(1)} %convert_element_type.110), kind=kOutput, calls=%fused_computation.4 | convolution fusion | flops 7824211968 | bytes 23824384 | tf_op jit(solution)/shard_map/dot_general | solution.py:142
  227.1 0.2 all-gather.2.cloned.1.call-start
  227.3 0.3 fusion.18
  227.6 33.2 %psum.30 = f32[1024]{0:T(1024)S(1)} all-reduce(f32[1024]{0:T(1024)S(1)} %fusion.18), channel_id=1, replica_groups=mesh['req'=16,'kv'=8] {'req'}, use_global_device_ids=true, to_apply=%region_10.11 | all-reduce | flops 1024 | bytes 8192 | tf_op jit(solution)/shard_map/psum | solution.py:130
  260.8 0.1 add_rsqrt_fusion
  260.9 101.0 %reduce-scatter.5.cloned.1.call-done = bf16[64,7424]{1,0:T(8,128)(2,1)} async-done(((bf16[1024,7424]{1,0:T(8,128)(2,1)}), bf16[64,7424]{1,0:T(8,128)(2,1)}) %reduce-scatter.5.cloned.1.call-update) | async-done | bytes 950288 | tf_op jit(solution)/shard_map/reduce_scatter | solution.py:141
  361.9 1.3 convert_element_type.113
  363.2 1.1 fusion.46
  364.3 0.0 all-reduce.7.cloned.1.call-start
  364.4 67.5 %all-gather.2.cloned.1.call-done = bf16[1024,3696]{1,0:T(8,128)(2,1)} async-done(((bf16[64,3696]{1,0:T(8,128)(2,1)}), bf16[1024,3696]{1,0:T(8,128)(2,1)}) %all-gather.2.cloned.1.call-update) | async-done | bytes 7569424 | tf_op jit(solution)/shard_map/all_gather | solution.py:152
  431.9 9.6 %convolution_convert_fusion.2 = bf16[1024,512]{1,0:T(8,128)(2,1)} fusion(bf16[1024,3696]{1,0:T(8,128)(2,1)} %all-gather.2.cloned.1.call-done, bf16[3696,512]{1,0:T(8,128)(2,1)} %param.28), kind=kOutput, calls=%fused_computation.32 | convolution fusion | flops 3876061184 | bytes 12402688 | tf_op jit(solution)/shard_map/dot_general | solution.py:151
  441.5 75.1 %all-reduce.7.cloned.1.call-done = bf16[1024,512]{1,0:T(8,128)(2,1)} async-done(((bf16[1024,512]{1,0:T(8,128)(2,1)}), bf16[1024,512]{1,0:T(8,128)(2,1)}) %all-reduce.7.cloned.1.call-update) | async-done | bytes 1048592 | tf_op jit(solution)/shard_map/psum | solution.py:154
  516.6 2.5 fusion.19
  (41 shorter events, 0.3 us)
Async XLA Ops:
  6.5 83.4 %copy-start = (bf16[1,8192,1,128]{3,1,2,0:T(8,128)(2,1)S(1)}, bf16[1,8192,1,128]{3,1,2,0:T(8,128)(2,1)}, u32[]{:S(2)}) copy-start(bf16[1,8192,1,128]{3,1,2,0:T(8,128)(2,1)} %param.32) | copy-start | bytes 6291460
  6.5 81.8 %reduce-scatter.3.cloned.1.call-start = ((), (), s32[]{:S(2)}) async-start(), calls=%async_computation.3 | async-start | bytes 2785280 | tf_op jit(solution)/shard_map/reduce_scatter | solution.py:71
  7.4 4.9 copy-start.8
  7.4 4.9 copy-start.4
  7.4 4.9 copy-start.9
  7.4 5.5 %copy-start.2 = (bf16[1024,512]{1,0:T(8,128)(2,1)S(1)}, bf16[1024,512]{1,0:T(8,128)(2,1)}, u32[]{:S(2)}) copy-start(bf16[1024,512]{1,0:T(8,128)(2,1)} %param.20) | copy-start | bytes 3145732
  7.4 45.7 %copy-start.6 = (s32[64]{0:T(128)S(1)}, s32[64]{0:T(128)}, u32[]{:S(2)}) copy-start(s32[64]{0:T(128)} %param.31) | copy-start | bytes 772
  12.2 198.7 %all-reduce.5.cloned.1.call-start = ((), (), s32[]{:S(2)}) async-start(), calls=%async_computation.4 | async-start | bytes 2097152 | tf_op jit(solution)/shard_map/psum | solution.py:127
  100.4 33.9 %copy-start.7 = (bf16[1024,512]{1,0:T(8,128)(2,1)S(1)}, bf16[1024,512]{1,0:T(8,128)(2,1)}, u32[]{:S(2)}) copy-start(bf16[1024,512]{1,0:T(8,128)(2,1)} %param.24) | copy-start | bytes 3145732
  134.4 2.3 copy-start.5
  134.4 76.5 %copy-start.3 = (bf16[1024,512]{1,0:T(8,128)(2,1)S(1)}, bf16[1024,512]{1,0:T(8,128)(2,1)}, u32[]{:S(2)}) copy-start(bf16[1024,512]{1,0:T(8,128)(2,1)} %param.20) | copy-start | bytes 3145732
  136.6 225.3 %reduce-scatter.5.cloned.1.call-start = ((), (), s32[]{:S(2)}) async-start(), calls=%async_computation.5 | async-start | bytes 16154624 | tf_op jit(solution)/shard_map/reduce_scatter | solution.py:141
  227.1 204.8 %all-gather.2.cloned.1.call-start = ((), (), s32[]{:S(2)}) async-start(), calls=%async_computation.6 | async-start | bytes 8077312 | tf_op jit(solution)/shard_map/all_gather | solution.py:152
  364.3 152.3 %all-reduce.7.cloned.1.call-start = ((), (), s32[]{:S(2)}) async-start(), calls=%async_computation.7 | async-start | bytes 2097152 | tf_op jit(solution)/shard_map/psum | solution.py:154
  431.9 87.2 %copy-start.1 = (bf16[1,8192,1,128]{3,1,2,0:T(8,128)(2,1)S(1)}, bf16[1,8192,1,128]{3,1,2,0:T(8,128)(2,1)}, u32[]{:S(2)}) copy-start(bf16[1,8192,1,128]{3,1,2,0:T(8,128)(2,1)} %param.32) | copy-start | bytes 6291460
Sparse Core Ops, SparseCore 0:
  12.3 75.9 reduce-scatter.2
  136.7 74.1 all-reduce.4
  227.2 134.6 reduce-scatter.4
  364.5 67.4 all-gather.1
  441.6 74.9 all-reduce.6
